TPU v7x, 32 devices: a whole 2x2x4 slice. The times are simulated.
32 devices in a mesh: walk: 4 (over x, core), chol: 8 (over z, y).
Axes of the slice: x: 2, y: 2, z: 4, core: 2. Of those that a mesh axis runs over, the one named last changes fastest.
Arguments:
- old_walkers: bfloat16 [96, 2048, 128], P(('walk', 'chol'))
- half_chol: bfloat16 [16, 128, 2048], P('chol'), may hold values from -0.1875 to 0.1875
- parent: int32 [192], P(('walk', 'chol')), may hold values from -1 to 11, as said below
- field: float32 [192, 2048], P(('walk', 'chol')), may hold values from -0.8 to 0.8
Outputs:
- new_walkers: bfloat16 [192, 2048, 128], P(('walk', 'chol'))
- energy: float32 [192], P(('walk', 'chol'))
Inputs may be any that keep to these rules, and one draw needn't show every extreme that they name: `parent`: the 4 devices that share an index of chol form a column. On each device the live slots (value >= 0) come first among its 6 slots, the rest hold -1. Each column has exactly 12 live slots, every device of it at least one, and some device of it has all 6 slots live. A live value m names the walker that the column's walk index m // 3 holds as its local walker m % 3.
All inputs are finite; a program needn't handle non-finite values.
Results may differ from a plain program's by a relative error of at most 0.0062.
Values may be sent and summed in bfloat16 or wider, within the bound.
No kernel may reach another device: no remote copies, remote signals or barrier semaphores. Data moves between devices by JAX's collectives and lax.ppermute only.
A program may use at most 192 MiB of HBM per device.

v0:
```python
import jax
import jax.numpy as jnp
from jax import lax
from jax.sharding import PartitionSpec as P

ITERS = 3


def green_half(walkers):
    widened = walkers.astype(jnp.float32)
    electrons = walkers.shape[2]
    intersection = widened[:, :electrons, :]
    identity = jnp.eye(electrons, dtype=jnp.float32)
    diagonal = jnp.diagonal(intersection, axis1=1, axis2=2)
    inverse = identity[None, :, :] / diagonal[:, None, :]
    for sweep in range(ITERS):
        product = jnp.einsum("wij,wjk->wik", intersection, inverse, precision=lax.Precision.HIGHEST)
        inverse = jnp.einsum(
            "wij,wjk->wik",
            inverse,
            2.0 * identity[None, :, :] - product,
            precision=lax.Precision.HIGHEST,
        )
    theta = jnp.einsum("wnk,wkj->wnj", widened, inverse, precision=lax.Precision.HIGHEST)
    return theta.astype(jnp.bfloat16)


def block_energy(theta, vectors):
    blocks = jnp.einsum("gin,wnj->wgij", vectors, theta, preferred_element_type=jnp.float32)
    traces = jnp.einsum("wgii->wg", blocks)
    crossed = jnp.sum(blocks * jnp.swapaxes(blocks, 2, 3), axis=(2, 3))
    return 0.5 * jnp.sum(traces * traces - crossed, axis=1)


def body(old_walkers, half_chol, parent, field):
    slot_dev = parent.shape[0]
    column = lax.all_gather(old_walkers, "walk", axis=0, tiled=True)
    living = parent >= 0
    source = jnp.maximum(parent, 0)
    kicked = (jnp.exp(field)[:, :, None] * column[source].astype(jnp.float32)).astype(jnp.bfloat16)
    new_walkers = jnp.where(living[:, None, None], kicked, jnp.zeros_like(kicked))
    theta = green_half(kicked)
    energy = jnp.zeros((slot_dev,), jnp.float32) + block_energy(
        theta, lax.all_gather(half_chol, "chol", axis=0, tiled=True)
    )
    energy = jnp.where(living, energy, 0.0)
    return (new_walkers, energy)


def solution(mesh):
    return jax.shard_map(
        body,
        mesh=mesh,
        in_specs=(
            P(("walk", "chol"), None, None),
            P("chol", None, None),
            P(("walk", "chol")),
            P(("walk", "chol"), None),
        ),
        out_specs=(P(("walk", "chol"), None, None), P(("walk", "chol"))),
        check_vma=False,
    )
```

profile of v0, /device:TPU:0, one launch (start us, length us, event | category | flops | bytes accessed | tf_op | source)
XLA Modules:
  0.0 217.5 jit_solution(15850261391445615935)
XLA Ops:
  7.2 0.0 all-gather.3.cloned.1.call-start
  7.2 0.7 all-gather.3.cloned.1.call-update
  7.9 0.0 all-gather.5.cloned.1.call-start
  7.9 0.7 all-gather.5.cloned.1.call-update
  8.6 0.9 exp.3
  9.5 0.7 broadcast_maximum_fusion
  10.2 0.6 iota_compare_fusion.1
  10.8 0.6 fusion.15
  11.4 0.7 fusion.16
  12.1 0.7 broadcast_compare_fusion
  12.7 45.9 %all-gather.3.cloned.1.call-done = bf16[12,2048,128]{2,1,0:T(8,128)(2,1)} async-done(((bf16[3,2048,128]{2,1,0:T(8,128)(2,1)}), bf16[12,2048,128]{2,1,0:T(8,128)(2,1)}) %all-gather.3.cloned.1.call-update) | async-done | bytes 6291472 | tf_op jit(solution)/shard_map/all_gather | solution.py:37
  58.7 5.5 %gather_fusion = bf16[6,2048,128]{2,1,0:T(8,128)(2,1)} fusion(bf16[12,2048,128]{2,1,0:T(8,128)(2,1)} %all-gather.3.cloned.1.call-done, s32[1024]{0:T(1024)S(1)} %pad_clamp_fusion), kind=kCustom, calls=%fused_computation | custom fusion | bytes 6291480 | tf_op jit(solution)/shard_map/gather | solution.py:40
  64.2 5.1 %broadcast_select_fusion = (bf16[6,2048,128]{2,1,0:T(8,128)(2,1)}, bf16[6,2048,128]{2,1,0:T(8,128)(2,1)S(1)}) fusion(pred[6]{0:T(512)(128)(4,1)S(1)} %broadcast_compare_fusion, bf16[6,2048,128]{2,1,0:T(8,128)(2,1)} %gather_fusion, f32[6,2048]{1,0:T(8,128)S(1)} %exp.3), kind=kLoop, calls=%fused_computation.11 | loop fusion | flops 6291456 | bytes 9486342 | tf_op jit(solution)/shard_map/jit(_where)/select_n | solution.py:41
  69.3 4.7 %copy.17 = f32[6,128,128]{0,2,1:T(8,128)} copy(f32[6,128,128]{2,1,0:T(8,128)S(1)} %slice_convert_fusion) | data formatting | bytes 786432 | tf_op jit(solution)/shard_map/slice | solution.py:12
  74.0 0.0 copy-start
  74.0 1.8 gather_fusion.1
  75.8 0.1 copy.18
  75.8 1.3 convolution_subtract_fusion.2
  77.1 1.4 fusion.5
  78.5 0.0 copy-done
  78.5 0.3 convolution_subtract_fusion.1
  78.9 0.5 fusion.17
  79.4 0.3 convolution_subtract_fusion
  79.7 0.5 fusion.18
  80.3 4.0 %convolution_convert_fusion = bf16[6,2048,128]{2,1,0:T(8,128)(2,1)} fusion(bf16[6,2048,128]{2,1,0:T(8,128)(2,1)S(1)} %get-tuple-element.7, f32[6,128,128]{2,1,0:T(8,128)S(1)} %fusion.18), kind=kOutput, calls=%fused_computation.9 | convolution fusion | flops 2417491968 | bytes 6684672 | tf_op jit(solution)/shard_map/wnk,wkj->wnj/dot_general | solution.py:24
  84.2 101.5 %all-gather.5.cloned.1.call-done = bf16[16,128,2048]{2,1,0:T(8,128)(2,1)} async-done(((bf16[2,128,2048]{2,1,0:T(8,128)(2,1)}), bf16[16,128,2048]{2,1,0:T(8,128)(2,1)}) %all-gather.5.cloned.1.call-update) | async-done | bytes 8388624 | tf_op jit(solution)/shard_map/all_gather | solution.py:44
  185.8 11.7 %fusion = f32[6,128,16,128]{3,1,2,0:T(8,128)} fusion(bf16[16,128,2048]{2,1,0:T(8,128)(2,1)} %all-gather.5.cloned.1.call-done, bf16[6,2048,128]{2,1,0:T(8,128)(2,1)} %convolution_convert_fusion), kind=kOutput, calls=%fused_computation.2 | convolution fusion | flops 6442450944 | bytes 17825792 | tf_op jit(solution)/shard_map/gin,wnj->wgij/dot_general | solution.py:29
  197.5 0.0 copy-start.1
  197.5 6.6 %copy.20 = f32[6,128,16,128]{1,3,2,0:T(8,128)} copy(f32[6,128,16,128]{3,1,2,0:T(8,128)} %fusion) | data formatting | bytes 12582912 | tf_op jit(solution)/shard_map/gin,wnj->wgij/dot_general | solution.py:29
  204.1 0.0 copy-done.1
  204.1 0.0 copy-start.2
  204.1 5.9 %fusion.3 = (f32[6,16]{1,0:T(8,128)S(1)}, f32[6,16]{1,0:T(8,128)S(1)}) fusion(f32[6,128,16,128]{1,3,2,0:T(8,128)} %copy.20, pred[128,128]{1,0:T(8,128)(4,1)S(1)} %copy-done.1, f32[6,128,16,128]{3,1,2,0:T(8,128)} %fusion), kind=kLoop, calls=%fused_computation.7 | loop fusion | flops 6291264 | bytes 12600064 | tf_op jit(solution)/shard_map/wgii->wg/reduce_sum | solution.py:30
  210.0 0.1 subtract_reduce_fusion
  210.1 0.0 copy-done.2
  210.1 0.5 multiply_select_fusion
  (3 shorter events, 0.0 us)
Async XLA Ops:
  7.2 51.5 %all-gather.3.cloned.1.call-start = ((), (), s32[]{:S(2)}) async-start(), calls=%async_computation | async-start | bytes 7864320 | tf_op jit(solution)/shard_map/all_gather | solution.py:37
  7.9 177.9 %all-gather.5.cloned.1.call-start = ((), (), s32[]{:S(2)}) async-start(), calls=%async_computation.1 | async-start | bytes 9437184 | tf_op jit(solution)/shard_map/all_gather | solution.py:44
  74.0 4.5 %copy-start = (f32[128,128]{1,0:T(8,128)S(1)}, f32[128,128]{1,0:T(8,128)}, u32[]{:S(2)}) copy-start(f32[128,128]{1,0:T(8,128)} %fusion.15) | copy-start | bytes 196612
  197.5 6.6 %copy-start.1 = (pred[128,128]{1,0:T(8,128)(4,1)S(1)}, pred[128,128]{1,0:T(8,128)(4,1)}, u32[]{:S(2)}) copy-start(pred[128,128]{1,0:T(8,128)(4,1)} %iota_compare_fusion.1) | copy-start | bytes 49156
  204.1 6.0 %copy-start.2 = (s32[6]{0:T(128)S(1)}, s32[6]{0:T(128)}, u32[]{:S(2)}) copy-start(s32[6]{0:T(128)} %param.6) | copy-start | bytes 76
Sparse Core Ops, SparseCore 0:
  9.6 49.0 all-gather.2
  60.8 124.9 all-gather.4
where the time goes:
time: 218 us; the launch traced here: 217 us
  waiting for transfers between devices  149 us (68%)
  matrix products  20.1 us (9%)
  local copies, waits for them, and re-layouts  19.5 us (9%)
  other arithmetic  14.8 us (7%)
  between operations  14.1 us (6%)
    all_gather x1, waiting for transfers between devices, body(): lax.all_gather(half_chol, 'chol', axis=0, tiled=True)  102 us
    all_gather x1, waiting for transfers between devices, body(): column = lax.all_gather(old_walkers, 'walk', axis=0, tiled=True)  45.9 us
    dot_general x1, matrix products, block_energy(): jnp.einsum('gin,wnj->wgij', vectors, theta, preferred_element_type=jnp.fl...  11.7 us
    dot_general x1, local copies, waits for them, and re-layouts, block_energy(): jnp.einsum('gin,wnj->wgij', vectors, theta, preferred_element_type=jnp.fl...  6.6 us
    reduce_sum x1, other arithmetic, block_energy(): traces = jnp.einsum('wgii->wg', blocks)  5.87 us
    gather x1, local copies, waits for them, and re-layouts, body(): column[source].astype(jnp.float32)  5.5 us
    select_n x1, other arithmetic, body(): jnp.where(living[:, None, None], kicked, jnp.zeros_like(kicked))  5.09 us
    slice x1, local copies, waits for them, and re-layouts, green_half(): intersection = widened[:, :electrons, :]  4.72 us
  transfers between devices with their start and end apart: 2, of which 2 were waited for; matrix products, arithmetic and copies ran while one was open for 14% of the time, Pallas kernels for 0%

commit v1 on v0

--- a/solution.py
+++ b/solution.py
@@ -2,8 +2,31 @@
 import jax.numpy as jnp
 from jax import lax
 from jax.sharding import PartitionSpec as P
+from jax.lax import axis_index, axis_size, ppermute
 
 ITERS = 3
+
+
+def _connect_flows(shard_in, out_dim):
+    found_now = list(shard_in.shape[1:])
+    found_now[out_dim] *= shard_in.shape[0]
+    arr_out = jnp.moveaxis(shard_in, 0, out_dim).reshape(found_now)
+    return arr_out
+
+
+def balance_loads_in(x_part, ax_name):
+    amount_of = axis_size(ax_name)
+    block_now = x_part[None]
+    for t in range(amount_of.bit_length() - 1):
+        shaped = 1 << t
+        b_now = ppermute(
+            block_now, axis_name=ax_name, perm=[(k0, k0 ^ shaped) for k0 in range(amount_of)]
+        )
+        newest = jnp.stack([block_now, b_now])
+        high = axis_index(ax_name)
+        value_now = high >> t & 1
+        block_now = jnp.where(value_now == 0, newest, newest[::-1]).reshape(-1, *x_part.shape)
+    return block_now
 
 
 def green_half(walkers):
@@ -34,7 +57,8 @@
 
 def body(old_walkers, half_chol, parent, field):
     slot_dev = parent.shape[0]
-    column = lax.all_gather(old_walkers, "walk", axis=0, tiled=True)
+    base_arr = balance_loads_in(old_walkers, "walk")
+    column = _connect_flows(base_arr, 0)
     living = parent >= 0
     source = jnp.maximum(parent, 0)
     kicked = (jnp.exp(field)[:, :, None] * column[source].astype(jnp.float32)).astype(jnp.bfloat16)

time: 218 us -> 170 us (0.78)
  waiting for transfers between devices: 149 us -> 88.7 us
  other arithmetic: 14.8 us -> 24.4 us
  starting transfers between devices: 0.08 us -> 3.42 us
    all_gather x1, waiting for transfers between devices: 102 us -> 18.1 us  [body(): lax.all_gather(half_chol, 'chol', axis=0, tiled=True)]
    ppermute x0 -> x2, waiting for transfers between devices: none -> 70 us  [balance_loads_in(): ppermute(block_now, axis_name=ax_name, perm=[(k0, k0 ^ shaped) for k0 in...]
    all_gather x1 -> x0, waiting for transfers between devices: 45.9 us -> none  [body(): column = lax.all_gather(old_walkers, 'walk', axis=0, tiled=True)]
    another operation x0 -> x3, other arithmetic: none -> 6.91 us  [balance_loads_in(): newest = jnp.stack([block_now, b_now])]
    select_n x0 -> x1, other arithmetic: none -> 4.05 us  [balance_loads_in(): jnp.where(value_now == 0, newest, newest[::-1]).reshape(-1, *x_part.shape)]
    ppermute x0 -> x2, starting transfers between devices: none -> 3.38 us  [balance_loads_in(): ppermute(block_now, axis_name=ax_name, perm=[(k0, k0 ^ shaped) for k0 in...]
  transfers between devices with their start and end apart: 2 -> 3, of which waited for: 2 -> 3; matrix products, arithmetic and copies ran while one was open for 14% -> 23% of each run, Pallas kernels for 0% -> 0%
where the time goes in v1:
time: 170 us; the launch traced here: 169 us
  waiting for transfers between devices  88.7 us (52%)
  other arithmetic  24.4 us (14%)
  matrix products  20.1 us (12%)
  local copies, waits for them, and re-layouts  18.6 us (11%)
  between operations  14.2 us (8%)
  starting transfers between devices  3.42 us (2%)
    ppermute x2, waiting for transfers between devices, balance_loads_in(): ppermute(block_now, axis_name=ax_name, perm=[(k0, k0 ^ shaped) for k0 in...  70 us
    all_gather x1, waiting for transfers between devices, body(): lax.all_gather(half_chol, 'chol', axis=0, tiled=True)  18.1 us
    dot_general x1, matrix products, block_energy(): jnp.einsum('gin,wnj->wgij', vectors, theta, preferred_element_type=jnp.fl...  11.7 us
    another operation x3, other arithmetic, balance_loads_in(): newest = jnp.stack([block_now, b_now])  6.91 us
    dot_general x1, local copies, waits for them, and re-layouts, block_energy(): jnp.einsum('gin,wnj->wgij', vectors, theta, preferred_element_type=jnp.fl...  6.58 us
    reduce_sum x1, other arithmetic, block_energy(): traces = jnp.einsum('wgii->wg', blocks)  5.87 us
    gather x1, local copies, waits for them, and re-layouts, body(): column[source].astype(jnp.float32)  5.5 us
    select_n x1, other arithmetic, body(): jnp.where(living[:, None, None], kicked, jnp.zeros_like(kicked))  5.05 us
  transfers between devices with their start and end apart: 3, of which 3 were waited for; matrix products, arithmetic and copies ran while one was open for 23% of the time, Pallas kernels for 0%

profile of v1, /device:TPU:0, one launch (start us, length us, event | category | flops | bytes accessed | tf_op | source)
XLA Modules:
  0.0 169.5 jit_solution(14174605143107208521)
XLA Ops:
  7.2 0.0 all-gather.2.cloned.1.call-start
  7.2 0.7 all-gather.2.cloned.1.call-update
  7.9 0.5 collective-permute-start
  8.4 3.2 %collective-permute-done = bf16[1,3,2048,128]{3,2,1,0:T(8,128)(2,1)S(1)} collective-permute-done((bf16[1,3,2048,128]{3,2,1,0:T(8,128)(2,1)}, bf16[1,3,2048,128]{3,2,1,0:T(8,128)(2,1)S(1)}, u32[]{:S(2)}, u32[]{:S(2)}) %collective-permute-start) | collective-permute-done | bytes 1572896 | tf_op jit(solution)/shard_map/ppermute | solution.py:22
  11.7 1.7 %pad_maximum_fusion.1 = bf16[2,1,3,2048,128]{4,3,2,1,0:T(8,128)(2,1)S(1)} fusion(bf16[1,1,3,2048,128]{4,3,2,1,0:T(8,128)(2,1)S(1)} %bitcast.41, bf16[1,1,3,2048,128]{4,3,2,1,0:T(8,128)(2,1)} %bitcast.40), kind=kLoop, calls=%fused_computation.13 | loop fusion | flops 1572864 | bytes 6291456 | tf_op jit(solution)/shard_map/stack | solution.py:25
  13.4 0.0 copy-start.2
  13.4 0.0 copy-start.3
  13.4 2.7 %fusion.6 = (bf16[1,2,3,2048,128]{4,3,2,1,0:T(8,128)(2,1)S(1)}, bf16[2,3,2048,128]{3,2,1,0:T(8,128)(2,1)}) fusion(bf16[2,1,3,2048,128]{4,3,2,1,0:T(8,128)(2,1)S(1)} %pad_maximum_fusion.1, pred[]{:T(512)S(6)} %eq.26), kind=kLoop, calls=%fused_computation.17 | loop fusion | flops 1572864 | bytes 9437185 | tf_op jit(solution)/shard_map/stack;reshape | solution.py:25
  16.1 2.9 %collective-permute-start.1 = (bf16[2,3,2048,128]{3,2,1,0:T(8,128)(2,1)}, bf16[2,3,2048,128]{3,2,1,0:T(8,128)(2,1)}, u32[]{:S(2)}, u32[]{:S(2)}) collective-permute-start(bf16[2,3,2048,128]{3,2,1,0:T(8,128)(2,1)} %get-tuple-element.9), channel_id=1, source_target_pairs={{0,16},{8,24},{16,0},{24,8},{1,17},{9,25},{17,1},{25,9},{2,18},{10... | collective-permute-start | bytes 9437192 | tf_op jit(solution)/shard_map/ppermute | solution.py:22
  19.0 0.0 copy-done.2
  19.0 0.0 copy-done.3
  19.1 0.6 iota_compare_fusion.1
  19.7 0.6 fusion.17
  20.3 0.6 fusion.18
  21.0 66.8 %collective-permute-done.1 = bf16[2,3,2048,128]{3,2,1,0:T(8,128)(2,1)} collective-permute-done((bf16[2,3,2048,128]{3,2,1,0:T(8,128)(2,1)}, bf16[2,3,2048,128]{3,2,1,0:T(8,128)(2,1)}, u32[]{:S(2)}, u32[]{:S(2)}) %collective-permute-start.1) | collective-permute-done | bytes 3145760 | tf_op jit(solution)/shard_map/ppermute | solution.py:22
  87.7 2.5 %pad_maximum_fusion = bf16[2,2,3,2048,128]{4,3,2,1,0:T(8,128)(2,1)S(1)} fusion(bf16[1,2,3,2048,128]{4,3,2,1,0:T(8,128)(2,1)} %bitcast.5, bf16[1,2,3,2048,128]{4,3,2,1,0:T(8,128)(2,1)S(1)} %get-tuple-element.8), kind=kLoop, calls=%fused_computation.5 | loop fusion | flops 3145728 | bytes 12582912 | tf_op jit(solution)/shard_map/stack | solution.py:25
  90.2 4.0 %reverse_select_fusion = bf16[2,2,3,2048,128]{4,3,2,1,0:T(8,128)(2,1)} fusion(bf16[2,2,3,2048,128]{4,3,2,1,0:T(8,128)(2,1)S(1)} %pad_maximum_fusion, pred[]{:T(512)S(6)} %eq.25), kind=kLoop, calls=%fused_computation.2 | loop fusion | flops 3145728 | bytes 12582913 | tf_op jit(solution)/shard_map/jit(_where)/select_n | solution.py:28
  94.2 5.5 %gather_fusion = bf16[6,2048,128]{2,1,0:T(8,128)(2,1)} fusion(bf16[12,2048,128]{2,1,0:T(8,128)(2,1)} %bitcast.38, s32[1024]{0:T(1024)S(1)} %pad_clamp_fusion), kind=kCustom, calls=%fused_computation | custom fusion | bytes 6291480 | tf_op jit(solution)/shard_map/gather | solution.py:64
  99.7 5.1 %broadcast_select_fusion = (bf16[6,2048,128]{2,1,0:T(8,128)(2,1)}, bf16[6,2048,128]{2,1,0:T(8,128)(2,1)S(1)}) fusion(pred[6]{0:T(512)(128)(4,1)S(1)} %broadcast_compare_fusion, bf16[6,2048,128]{2,1,0:T(8,128)(2,1)} %gather_fusion, f32[6,2048]{1,0:T(8,128)S(1)} %exp.3), kind=kLoop, calls=%fused_computation.15 | loop fusion | flops 6291456 | bytes 9486342 | tf_op jit(solution)/shard_map/jit(_where)/select_n | solution.py:65
  104.8 4.7 %copy.17 = f32[6,128,128]{0,2,1:T(8,128)} copy(f32[6,128,128]{2,1,0:T(8,128)S(1)} %slice_convert_fusion) | data formatting | bytes 786432 | tf_op jit(solution)/shard_map/slice | solution.py:35
  109.5 0.0 copy-start
  109.5 1.8 %gather_fusion.1 = f32[128,6]{1,0:T(8,128)S(1)} fusion(f32[6,128,128]{0,2,1:T(8,128)} %copy.17, s32[128]{0:T(128)S(1)} %or_bitcast_fusion), kind=kCustom, calls=%fused_computation.1 | custom fusion | bytes 7168 | tf_op jit(solution)/shard_map/jit(diagonal)/gather | solution.py:37
  111.3 0.1 copy.18
  111.3 1.3 convolution_subtract_fusion.2
  112.6 1.4 fusion.7
  114.0 0.0 copy-done
  114.0 0.3 convolution_subtract_fusion.1
  114.4 0.5 fusion.19
  114.9 0.3 convolution_subtract_fusion
  115.2 0.5 fusion.20
  115.8 3.9 %convolution_convert_fusion = bf16[6,2048,128]{2,1,0:T(8,128)(2,1)} fusion(bf16[6,2048,128]{2,1,0:T(8,128)(2,1)S(1)} %get-tuple-element.7, f32[6,128,128]{2,1,0:T(8,128)S(1)} %fusion.20), kind=kOutput, calls=%fused_computation.12 | convolution fusion | flops 2417491968 | bytes 6684672 | tf_op jit(solution)/shard_map/wnk,wkj->wnj/dot_general | solution.py:47
  119.7 18.1 %all-gather.2.cloned.1.call-done = bf16[16,128,2048]{2,1,0:T(8,128)(2,1)} async-done(((bf16[2,128,2048]{2,1,0:T(8,128)(2,1)}), bf16[16,128,2048]{2,1,0:T(8,128)(2,1)}) %all-gather.2.cloned.1.call-update) | async-done | bytes 8388624 | tf_op jit(solution)/shard_map/all_gather | solution.py:68
  137.8 11.7 %fusion = f32[6,128,16,128]{3,1,2,0:T(8,128)} fusion(bf16[16,128,2048]{2,1,0:T(8,128)(2,1)} %all-gather.2.cloned.1.call-done, bf16[6,2048,128]{2,1,0:T(8,128)(2,1)} %convolution_convert_fusion), kind=kOutput, calls=%fused_computation.3 | convolution fusion | flops 6442450944 | bytes 17825792 | tf_op jit(solution)/shard_map/gin,wnj->wgij/dot_general | solution.py:52
  149.5 0.0 copy-start.1
  149.5 6.6 %copy.20 = f32[6,128,16,128]{1,3,2,0:T(8,128)} copy(f32[6,128,16,128]{3,1,2,0:T(8,128)} %fusion) | data formatting | bytes 12582912 | tf_op jit(solution)/shard_map/gin,wnj->wgij/dot_general | solution.py:52
  156.1 0.0 copy-done.1
  156.1 5.9 %fusion.3 = (f32[6,16]{1,0:T(8,128)S(1)}, f32[6,16]{1,0:T(8,128)S(1)}) fusion(f32[6,128,16,128]{1,3,2,0:T(8,128)} %copy.20, pred[128,128]{1,0:T(8,128)(4,1)S(1)} %copy-done.1, f32[6,128,16,128]{3,1,2,0:T(8,128)} %fusion), kind=kLoop, calls=%fused_computation.9 | loop fusion | flops 6291264 | bytes 12600064 | tf_op jit(solution)/shard_map/wgii->wg/reduce_sum | solution.py:53
  162.0 0.1 subtract_reduce_fusion
  162.1 0.5 multiply_select_fusion
  (6 shorter events, 0.1 us)
Async XLA Ops:
  7.2 130.6 %all-gather.2.cloned.1.call-start = ((), (), s32[]{:S(2)}) async-start(), calls=%async_computation | async-start | bytes 9437184 | tf_op jit(solution)/shard_map/all_gather | solution.py:68
  7.9 3.8 %collective-permute-start = (bf16[1,3,2048,128]{3,2,1,0:T(8,128)(2,1)}, bf16[1,3,2048,128]{3,2,1,0:T(8,128)(2,1)S(1)}, u32[]{:S(2)}, u32[]{:S(2)}) collective-permute-start(bf16[1,3,2048,128]{3,2,1,0:T(8,128)(2,1)} %bitcast.39), channel_id=1, source_target_pairs={{0,8},{8,0},{16,24},{24,16},{1,9},{9,1},{17,25},{25,17},{2,10},{10... | collective-permute-start | bytes 4718600 | tf_op jit(solution)/shard_map/ppermute | solution.py:22
  13.4 5.6 %copy-start.2 = (f32[6,2048]{1,0:T(8,128)S(1)}, f32[6,2048]{1,0:T(8,128)}, u32[]{:S(2)}) copy-start(f32[6,2048]{1,0:T(8,128)} %param.7) | copy-start | bytes 147460
  13.4 5.7 %copy-start.3 = (s32[6]{0:T(128)S(1)}, s32[6]{0:T(128)}, u32[]{:S(2)}) copy-start(s32[6]{0:T(128)} %param.6) | copy-start | bytes 76
  16.1 71.6 %collective-permute-start.1 = (bf16[2,3,2048,128]{3,2,1,0:T(8,128)(2,1)}, bf16[2,3,2048,128]{3,2,1,0:T(8,128)(2,1)}, u32[]{:S(2)}, u32[]{:S(2)}) collective-permute-start(bf16[2,3,2048,128]{3,2,1,0:T(8,128)(2,1)} %get-tuple-element.9), channel_id=1, source_target_pairs={{0,16},{8,24},{16,0},{24,8},{1,17},{9,25},{17,1},{25,9},{2,18},{10... | collective-permute-start | bytes 9437192 | tf_op jit(solution)/shard_map/ppermute | solution.py:22
  109.5 4.5 %copy-start = (f32[128,128]{1,0:T(8,128)S(1)}, f32[128,128]{1,0:T(8,128)}, u32[]{:S(2)}) copy-start(f32[128,128]{1,0:T(8,128)} %fusion.17) | copy-start | bytes 196612
  149.5 6.6 %copy-start.1 = (pred[128,128]{1,0:T(8,128)(4,1)S(1)}, pred[128,128]{1,0:T(8,128)(4,1)}, u32[]{:S(2)}) copy-start(pred[128,128]{1,0:T(8,128)(4,1)} %iota_compare_fusion.1) | copy-start | bytes 49156
Sparse Core Ops, SparseCore 0:
  10.1 127.6 all-gather.1
